TPU v7x, 256 devices: a whole 4x4x8 slice. The times are simulated.
256 devices in a mesh: group: 8 (over x, core), inner: 32 (over z, y).
Axes of the slice: x: 4, y: 4, z: 8, core: 2. Of those that a mesh axis runs over, the one named last changes fastest.
Arguments:
- flow_field: float32 [1536, 1536, 128], P('inner', 'group'), may hold values from -6 to 6
- sketch_rows: float32 [1536, 128], P('inner'), may hold values from -6 to 6
- sketch_cols: float32 [1536, 128], P('group'), may hold values from -6 to 6
- sketch_depth: float32 [128, 128], replicated, may hold values from -6 to 6
- bit_widths: int32 [2], replicated, may hold values from 6 to 8
- bin_edges: int32 [9], replicated, may hold values from -6 to 6, as said below
Outputs:
- basis_one: float32 [1536, 128], P('inner')
- basis_two: float32 [1536, 128], P('group')
- core: float32 [128, 128, 128], P('inner', 'group')
- residual: float32 [2, 128, 128, 128], P(None, 'inner', 'group')
- energy: float32 [2, 1536, 128], P(None, 'inner')
- histogram: float32 [2, 1536, 8], P(None, 'inner')
Inputs may be any that keep to these rules, and one draw needn't show every extreme that they name: `bin_edges`: strictly increasing; the first is -6 and the last 6.
All inputs are finite; a program needn't handle non-finite values.
Results may differ from a plain program's by a relative error of at most 0.0008.
Values sent between devices are 32-bit elements; how exact they have to be, the bound alone decides.
No kernel may reach another device: no remote copies, remote signals or barrier semaphores. Data moves between devices by JAX's collectives and lax.ppermute only.
A program may use at most 128 MiB of HBM per device.

v0:
```python
import math

import jax
import jax.numpy as jnp
from jax import lax
from jax.sharding import PartitionSpec as P

N1 = 1536
N2 = 1536
N3 = 128
R = 128
NEDGE = 9
NBINS = 8


precise = lax.Precision.HIGHEST
two_pi = 2.0 * 3.141592653589793
error_boost = 16.0


def gram_of(sketch):
    return jnp.dot(sketch.T, sketch, precision=precise)


def orthonormal_rows(sketch, gram_matrix):
    lower_factor = jnp.linalg.cholesky(gram_matrix)
    return jax.scipy.linalg.solve_triangular(lower_factor, sketch.T, lower=True).T


def soft_residual(core_values, step_size):
    return -jnp.sin(two_pi * core_values[None] / step_size[:, None, None, None]) / two_pi


def local(flow_field, sketch_rows, sketch_cols, sketch_depth, bit_widths, bin_edges):
    reduced = jnp.einsum("ijk,kr->ijr", flow_field, sketch_depth, precision=precise)
    mode_one = jnp.einsum("ijr,jr->ir", reduced, sketch_cols, precision=precise)
    mode_two = jnp.einsum("ijr,ir->jr", reduced, sketch_rows, precision=precise)
    mode_one = lax.psum(mode_one, "group")
    basis_one = orthonormal_rows(mode_one, lax.psum(gram_of(mode_one), "inner"))
    mode_two = lax.psum(mode_two, "inner")
    basis_two = orthonormal_rows(mode_two, lax.psum(gram_of(mode_two), "group"))
    along_two = jnp.einsum("ijk,js->isk", flow_field, basis_two, precision=precise)
    levels = jnp.exp2(bit_widths.astype(jnp.float32) - 1.0) - 1.0
    summed_two = lax.psum_scatter(along_two, "group", scatter_dimension=1, tiled=True)
    partial_rows = jnp.einsum("ir,isk->rsk", basis_one, summed_two, precision=precise)
    core_shard = lax.psum_scatter(partial_rows, "inner", scatter_dimension=0, tiled=True)
    peak = lax.pmax(jnp.max(jnp.abs(core_shard)), ("group", "inner"))
    residual_shard = soft_residual(core_shard, peak / levels)
    spread = lax.all_gather(residual_shard, "group", axis=2, tiled=True)
    mixed_core = jnp.einsum(
        "ir,brsk->bisk",
        basis_one,
        lax.all_gather(spread, "inner", axis=1, tiled=True),
        precision=precise,
    )
    error_scale = error_boost * math.sqrt(N1 * N2) / R
    field_error = error_scale * jnp.einsum(
        "bisk,js->bijk", mixed_core, basis_two, precision=precise
    )
    energy_part = jnp.sum(field_error * field_error, axis=2) / N2
    edge_values = bin_edges.astype(jnp.float32)
    ramp_part = jnp.stack(
        [
            jnp.sum(jnp.clip(field_error - edge_values[index_edge] + 0.5, 0.0, 1.0), axis=(2, 3))
            for index_edge in range(NEDGE)
        ],
        axis=-1,
    )
    energy, ramp_sums = lax.psum((energy_part, ramp_part), "group")
    histogram = (ramp_sums[..., :-1] - ramp_sums[..., 1:]) * (NBINS / (N2 * N3))
    return (basis_one, basis_two, core_shard, residual_shard, energy, histogram)


def solution(mesh):
    in_specs = (P("inner", "group", None), P("inner", None), P("group", None), P(), P(), P())
    out_specs = (
        P("inner", None),
        P("group", None),
        P("inner", "group", None),
        P(None, "inner", "group", None),
        P(None, "inner", None),
        P(None, "inner", None),
    )
    return jax.shard_map(local, mesh=mesh, in_specs=in_specs, out_specs=out_specs, check_vma=False)
```

profile of v0, /device:TPU:1, one launch (start us, length us, event | category | flops | bytes accessed | tf_op | source)
XLA Modules:
  0.0 862.9 jit_solution(15359649875850458368)
XLA Ops:
  7.2 0.0 copy-start
  7.2 0.0 copy-start.5
  7.2 0.0 all-reduce.7.cloned.1.call-start
  7.2 0.8 copy-done
  8.0 7.1 multiply_reduce_fusion.2
  15.1 0.1 copy.31
  15.2 24.0 %psum.42 = f32[48,128]{0,1:T(8,128)S(1)} all-reduce(f32[48,128]{0,1:T(8,128)S(1)} %bitcast.98), channel_id=1, replica_groups=mesh['group'=8,'inner'=32] {'group'}, use_global_device_ids=true, to_apply=%region_0.0 | all-reduce | flops 6144 | bytes 49152 | tf_op jit(solution)/shard_map/psum | solution.py:38
  39.2 0.9 fusion.25
  40.1 0.0 copy-done.5
  40.1 2.8 multiply_reduce_fusion.1
  42.9 0.8 copy.39
  43.7 0.0 all-reduce.7.cloned.1.call-update
  43.7 0.0 all-reduce.5.cloned.1.call-start
  43.7 143.6 %all-reduce.7.cloned.1.call-done = (f32[128,128]{0,1:T(8,128)}, f32[192,128]{0,1:T(8,128)}) async-done(((f32[128,128]{0,1:T(8,128)}, f32[192,128]{0,1:T(8,128)}), (f32[128,128]{0,1:T(8,128)}, f32[192,128]{0,1:T(8,128)})) %all-reduce.7.cloned.1.call-update) | async-done | bytes 163856 | tf_op jit(solution)/shard_map/psum | solution.py:39
  187.3 1.9 fusion.26
  189.2 0.0 all-reduce.5.cloned.1.call-update
  189.2 0.2 reduce-scatter.3.cloned.1.call-start
  189.5 65.3 %all-reduce.5.cloned.1.call-done = f32[128,128]{0,1:T(8,128)} async-done(((f32[128,128]{0,1:T(8,128)}), f32[128,128]{0,1:T(8,128)}) %all-reduce.5.cloned.1.call-update) | async-done | bytes 65552 | tf_op jit(solution)/shard_map/psum | solution.py:41
  254.8 0.9 copy.22
  255.7 0.9 fusion.14
  256.6 11.7 %cholesky.55 = f32[128,128]{1,0:T(8,128)S(1)} custom-call(f32[128,128]{1,0:T(8,128)S(1)} %fusion.14), custom_call_target="Cholesky" | custom-call | tf_op jit(solution)/shard_map/jit(cholesky)/cholesky | solution.py:26
  268.3 0.6 compare_reduce_fusion
  269.0 0.7 fusion.11
  269.6 9.8 %custom-call.11 = f32[1,128,128]{1,2,0:T(8,128)S(1)} custom-call(f32[1,128,128]{2,1,0:T(8,128)S(1)} %fusion.11), custom_call_target="InvertDiagBlocksLowerTriangular" | custom-call | tf_op jit(solution)/shard_map/jit(_solve_triangular)/triangular_solve | solution.py:27
  279.5 1.3 fusion.12
  280.7 0.0 copy-start.1
  280.7 0.0 copy-start.6
  280.8 4.8 fusion.6
  285.6 0.0 copy-start.7
  285.6 3.5 copy.57
  289.1 0.0 reduce-scatter.3.cloned.1.call-update
  289.1 0.3 reduce-scatter.5.cloned.1.call-start
  289.4 0.0 copy-done.3
  289.4 0.1 copy.20
  289.5 11.7 %cholesky.44 = f32[128,128]{1,0:T(8,128)S(1)} custom-call(f32[128,128]{1,0:T(8,128)S(1)} %fusion.17), custom_call_target="Cholesky" | custom-call | tf_op jit(solution)/shard_map/jit(cholesky)/cholesky | solution.py:26
  301.3 0.6 compare_reduce_fusion.1
  301.9 0.7 fusion.10
  302.6 9.8 %custom-call.10 = f32[1,128,128]{1,2,0:T(8,128)S(1)} custom-call(f32[1,128,128]{2,1,0:T(8,128)S(1)} %fusion.10), custom_call_target="InvertDiagBlocksLowerTriangular" | custom-call | tf_op jit(solution)/shard_map/jit(_solve_triangular)/triangular_solve | solution.py:27
  312.4 0.3 fusion.15
  312.7 0.0 copy-start.4
  312.7 13.7 %reduce-scatter.3.cloned.1.call-done = f32[48,16,128]{2,0,1:T(8,128)} async-done(((f32[48,128,128]{2,0,1:T(8,128)}), f32[48,16,128]{2,0,1:T(8,128)}) %reduce-scatter.3.cloned.1.call-update) | async-done | bytes 393232 | tf_op jit(solution)/shard_map/reduce_scatter | solution.py:44
  326.4 2.0 fusion.21
  328.4 1.6 copy.23
  330.0 0.0 reduce-scatter.5.cloned.1.call-update
  330.1 0.0 all-gather.2.cloned.1.call-start
  330.1 213.5 %reduce-scatter.5.cloned.1.call-done = f32[4,16,128]{2,1,0:T(8,128)} async-done(((f32[128,16,128]{2,1,0:T(8,128)}), f32[4,16,128]{2,1,0:T(8,128)}) %reduce-scatter.5.cloned.1.call-update) | async-done | bytes 32784 | tf_op jit(solution)/shard_map/reduce_scatter | solution.py:46
  543.6 1.4 broadcast_multiply_fusion.2
  545.0 79.6 %pmax.7 = f32[]{:T(128)} all-reduce(f32[]{:T(128)} %get-tuple-element.34), channel_id=1, replica_groups=mesh['group'=8,'inner'=32] {'group','inner'}, use_global_device_ids=true, to_apply=%region_9.11 | all-reduce | flops 1 | bytes 8 | tf_op jit(solution)/shard_map/pmax | solution.py:47
  624.7 0.0 copy-done.6
  624.7 0.7 add_divide_fusion
  625.3 0.3 fusion.9
  625.6 0.0 copy-start.2
  625.6 14.9 %all_gather.6 = f32[2,4,128,128]{3,2,1,0:T(8,128)} all-gather(f32[2,4,16,128]{3,2,1,0:T(8,128)S(1)} %fusion.9), channel_id=1, replica_groups=mesh['group'=8,'inner'=32] {'group'}, dimensions={2}, use_global_device_ids=true | all-gather | bytes 589824 | tf_op jit(solution)/shard_map/all_gather | solution.py:49
  640.6 0.0 all-gather.2.cloned.1.call-update
  640.6 0.0 copy-done.7
  640.6 0.7 fusion.24
  641.3 134.7 %all-gather.2.cloned.1.call-done = f32[2,128,128,128]{3,2,1,0:T(8,128)} async-done(((f32[2,4,128,128]{3,2,1,0:T(8,128)}), f32[2,128,128,128]{3,2,1,0:T(8,128)}) %all-gather.2.cloned.1.call-update) | async-done | bytes 16777232 | tf_op jit(solution)/shard_map/all_gather | solution.py:53
  776.1 22.9 %fusion = f32[2,128,128,48]{2,3,1,0:T(8,128)S(1)} fusion(f32[2,128,128,128]{3,2,1,0:T(8,128)} %all-gather.2.cloned.1.call-done, f32[128,48]{0,1:T(8,128)S(1)} %fusion.15), kind=kOutput, calls=%fused_computation | convolution fusion | flops 2415919104 | bytes 23093248 | tf_op jit(solution)/shard_map/ir,brsk->bisk/dot_general | solution.py:50
  799.0 0.0 copy-done.4
  799.0 0.0 copy-done.2
  799.0 0.0 copy-done.1
  799.0 32.9 %clamp_reduce_fusion = (f32[2,48]{1,0:T(2,128)S(1)}, f32[2,48]{1,0:T(2,128)S(1)}, f32[2,48]{1,0:T(2,128)S(1)}, f32[2,48]{1,0:T(2,128)S(1)}, f32[2,48]{1,0:T(2,12...) fusion(f32[]{:T(128)} %bitcast.39, f32[]{:T(128)} %bitcast.23, ...), kind=kOutput, calls=%fused_computation.2 | convolution fusion | flops 3715877888 | bytes 6442404 | tf_op jit(solution)/shard_map/bisk,js->bijk/dot_general | solution.py:57
  832.0 23.8 %all-reduce.1 = (f32[2,48,128]{2,1,0:T(8,128)}, f32[2,48,9]{1,0,2:T(2,128)S(1)}) all-reduce(f32[2,48,128]{2,1,0:T(8,128)S(1)} %broadcast_multiply_fusion.1, f32[2,48,9]{1,0,2:T(2,128)S(1)} %constant_dynamic-update-slice_fusion), channel_id=1, replica_groups=mesh['group'=8,'inner'=32] {'group'}, use_global_device_ids=true, to_apply=%region_11.13 | all-reduce | flops 13152 | bytes 105216 | tf_op jit(solution)/shard_map/psum | solution.py:69
  855.8 0.6 copy.24
  (16 shorter events, 0.2 us)
Async XLA Ops:
  7.2 0.8 copy-start
  7.2 33.0 %copy-start.5 = (f32[48,128]{1,0:T(8,128)S(1)}, f32[48,128]{1,0:T(8,128)}, u32[]{:S(2)}) copy-start(f32[48,128]{1,0:T(8,128)} %param.8) | copy-start | bytes 73732
  7.2 180.1 %all-reduce.7.cloned.1.call-start = ((), (), s32[]{:S(2)}) async-start(), calls=%async_computation.6 | async-start | bytes 393216 | tf_op jit(solution)/shard_map/psum | solution.py:39
  43.7 211.1 %all-reduce.5.cloned.1.call-start = ((), (), s32[]{:S(2)}) async-start(), calls=%async_computation.2 | async-start | bytes 131072 | tf_op jit(solution)/shard_map/psum | solution.py:41
  187.3 102.1 %copy-start.3 = (f32[128,128]{0,1:T(8,128)S(1)}, f32[128,128]{0,1:T(8,128)}, u32[]{:S(2)}) copy-start(f32[128,128]{0,1:T(8,128)} %get-tuple-element.29) | copy-start | bytes 196612
  189.2 137.2 %reduce-scatter.3.cloned.1.call-start = ((), (), s32[]{:S(2)}) async-start(), calls=%async_computation.3 | async-start | bytes 3538944 | tf_op jit(solution)/shard_map/reduce_scatter | solution.py:44
  280.7 518.3 %copy-start.1 = (f32[128,192]{0,1:T(8,128)}, f32[128,192]{0,1:T(8,128)S(1)}, u32[]{:S(2)}) copy-start(f32[128,192]{0,1:T(8,128)S(1)} %fusion.12) | copy-start | bytes 294916
  280.7 343.9 %copy-start.6 = (s32[2]{0:T(128)S(1)}, s32[2]{0:T(128)}, u32[]{:S(2)}) copy-start(s32[2]{0:T(128)} %param.11) | copy-start | bytes 28
  285.6 355.0 %copy-start.7 = (s32[9]{0:T(128)S(1)}, s32[9]{0:T(128)}, u32[]{:S(2)}) copy-start(s32[9]{0:T(128)} %param.12) | copy-start | bytes 112
  289.1 254.5 %reduce-scatter.5.cloned.1.call-start = ((), (), s32[]{:S(2)}) async-start(), calls=%async_computation.4 | async-start | bytes 1081344 | tf_op jit(solution)/shard_map/reduce_scatter | solution.py:46
  312.7 486.3 %copy-start.4 = (f32[128,48]{0,1:T(8,128)}, f32[128,48]{0,1:T(8,128)S(1)}, u32[]{:S(2)}) copy-start(f32[128,48]{0,1:T(8,128)S(1)} %fusion.15) | copy-start | bytes 73732
  330.1 446.0 %all-gather.2.cloned.1.call-start = ((), (), s32[]{:S(2)}) async-start(), calls=%async_computation.5 | async-start | bytes 17301504 | tf_op jit(solution)/shard_map/all_gather | solution.py:53
  625.6 173.3 %copy-start.2 = (f32[2,4,16,128]{3,2,1,0:T(8,128)}, f32[2,4,16,128]{3,2,1,0:T(8,128)S(1)}, u32[]{:S(2)}) copy-start(f32[2,4,16,128]{3,2,1,0:T(8,128)S(1)} %fusion.9) | copy-start | bytes 196612
Sparse Core Ops, SparseCore 0:
  43.8 143.4 all-reduce.6
  190.2 64.5 all-reduce.4
  289.3 37.1 reduce-scatter.2
  330.7 212.9 reduce-scatter.4
  640.7 135.2 all-gather.1
where the time goes:
time: 864 us; the launch traced here: 863 us
  waiting for transfers between devices  571 us (66%)
  blocking collectives  142 us (16%)
  matrix products  74.1 us (9%)
  other arithmetic  51.7 us (6%)
  between operations  14 us (2%)
  local copies, waits for them, and re-layouts  9.15 us (1%)
    reduce_scatter x1, waiting for transfers between devices, local(): lax.psum_scatter(partial_rows, 'inner', scatter_dimension=0, tiled=True)  214 us
    psum x1, waiting for transfers between devices, local(): basis_one = orthonormal_rows(mode_one, lax.psum(gram_of(mode_one), 'inner'))  144 us
    all_gather x1, waiting for transfers between devices, local(): lax.all_gather(spread, 'inner', axis=1, tiled=True)  135 us
    pmax x1, blocking collectives, local(): peak = lax.pmax(jnp.max(jnp.abs(core_shard)), ('group', 'inner'))  79.6 us
    psum x1, waiting for transfers between devices, local(): basis_two = orthonormal_rows(mode_two, lax.psum(gram_of(mode_two), 'group'))  65.3 us
    dot_general x1, matrix products, local(): jnp.einsum('bisk,js->bijk', mixed_core, basis_two, precision=precise)  32.9 us
    another operation x6, other arithmetic, orthonormal_rows(): lower_factor = jnp.linalg.cholesky(gram_matrix)  24.8 us
    psum x1, blocking collectives, local(): mode_one = lax.psum(mode_one, 'group')  24 us
  transfers between devices with their start and end apart: 5, of which 5 were waited for; matrix products, arithmetic and copies ran while one was open for 3% of the time, Pallas kernels for 0%

commit v1 on v0

v1 whole, which is shorter than its diff:
```python
import math

import jax
import jax.numpy as jnp
from jax import lax
from jax.sharding import PartitionSpec as P

NEDGE = 9
NBINS = 8


precise = lax.Precision.HIGHEST
two_pi = 2.0 * 3.141592653589793
error_boost = 16.0


def gram_of(sketch):
    return jnp.dot(sketch.T, sketch, precision=precise)


def orthonormal_rows(sketch, gram_matrix):
    lower_factor = jnp.linalg.cholesky(gram_matrix)
    return jax.scipy.linalg.solve_triangular(lower_factor, sketch.T, lower=True).T


def soft_residual(core_values, step_size):
    shape = (-1,) + (1,) * core_values.ndim
    return -jnp.sin(two_pi * core_values[None] / step_size.reshape(shape)) / two_pi


def xor_pairs(n, d):
    return [(a, a ^ d) for a in range(n)]


def bits_of(n):
    return [1 << t for t in range(n.bit_length() - 1)]


def all_reduce(x, axis, n, op=jnp.add):
    for d in bits_of(n):
        x = op(x, lax.ppermute(x, axis, xor_pairs(n, d)))
    return x


def reduce_scatter(x, axis, n):
    idx = lax.axis_index(axis)
    nb = n.bit_length() - 1
    chunk = x.shape[0] // n
    rest = x.shape[1:]
    x = x.reshape((2,) * nb + (chunk,) + rest)
    left = list(range(nb))
    for d in bits_of(n):
        t = left.index(nb - 1 - (d.bit_length() - 1))
        bit = (idx // d) % 2
        keep = lax.dynamic_index_in_dim(x, bit, axis=t, keepdims=False)
        send = lax.dynamic_index_in_dim(x, 1 - bit, axis=t, keepdims=False)
        x = keep + lax.ppermute(send, axis, xor_pairs(n, d))
        left.pop(t)
    return x.reshape((chunk,) + rest)


def all_gather(x, axis, n):
    idx = lax.axis_index(axis)
    nb = n.bit_length() - 1
    chunk = x.shape[0]
    rest = x.shape[1:]
    have = []
    for d in reversed(bits_of(n)):
        pos = nb - 1 - (d.bit_length() - 1)
        t = sum(1 for h in have if h < pos)
        other = lax.ppermute(x, axis, xor_pairs(n, d))
        bit = (idx // d) % 2
        x = jnp.where(bit == 0, jnp.stack([x, other], axis=t), jnp.stack([other, x], axis=t))
        have.append(pos)
        have.sort()
    return x.reshape((n * chunk,) + rest)


def make_local(n_group, n_inner):
    def local(flow_field, sketch_rows, sketch_cols, sketch_depth, bit_widths, bin_edges):
        rows_i, cols_j, depth_k = flow_field.shape
        rank = sketch_depth.shape[1]
        n1 = rows_i * n_inner
        n2 = cols_j * n_group
        k_blk = depth_k // n_group
        r_blk = rank // n_inner
        s_blk = rank // n_group
        g = lax.axis_index("group")
        p = lax.axis_index("inner")

        reduced = jnp.einsum("ijk,kr->ijr", flow_field, sketch_depth, precision=precise)
        mode_one = jnp.einsum("ijr,jr->ir", reduced, sketch_cols, precision=precise)
        mode_two = jnp.einsum("ijr,ir->jr", reduced, sketch_rows, precision=precise)
        mode_one = all_reduce(mode_one, "group", n_group)
        mode_two = all_reduce(mode_two, "inner", n_inner)
        basis_one = orthonormal_rows(mode_one, all_reduce(gram_of(mode_one), "inner", n_inner))
        basis_two = orthonormal_rows(mode_two, all_reduce(gram_of(mode_two), "group", n_group))
        basis_two_all = all_gather(basis_two, "group", n_group)

        along_two = jnp.einsum("ijk,js->kis", flow_field, basis_two, precision=precise)
        along_two = reduce_scatter(along_two, "group", n_group)
        partial = jnp.einsum("kis,ir->krs", along_two, basis_one, precision=precise)
        partial = partial.reshape(k_blk * rank, rank)
        core_part = reduce_scatter(partial, "inner", n_inner)
        peak = all_reduce(jnp.max(jnp.abs(core_part)), "inner", n_inner, jnp.maximum)
        peak = all_reduce(peak, "group", n_group, jnp.maximum)
        core_k = all_gather(core_part, "inner", n_inner).reshape(k_blk, rank, rank)

        levels = jnp.exp2(bit_widths.astype(jnp.float32) - 1.0) - 1.0
        step = peak / levels
        residual_k = soft_residual(core_k, step)

        core_rows = lax.dynamic_slice_in_dim(core_k, p * r_blk, r_blk, axis=1)
        core_rows = all_gather(core_rows, "group", n_group)
        core_block = lax.dynamic_slice_in_dim(core_rows, g * s_blk, s_blk, axis=2)
        core_block = jnp.transpose(core_block, (1, 2, 0))
        residual_block = soft_residual(core_block, step)

        mixed = jnp.einsum("ir,bkrs->sbik", basis_one, residual_k, precision=precise)
        nb = mixed.shape[1]
        mixed = mixed.reshape(rank, nb * rows_i * k_blk)
        error_scale = error_boost * math.sqrt(n1 * n2) / rank
        field_error = error_scale * jnp.dot(basis_two_all, mixed, precision=precise)
        energy_part = (jnp.sum(field_error * field_error, axis=0) / n2).reshape(nb, rows_i, k_blk)
        edge_values = bin_edges.astype(jnp.float32)
        ramp_part = jnp.stack(
            [
                jnp.sum(
                    jnp.clip(field_error - edge_values[index_edge] + 0.5, 0.0, 1.0), axis=0
                ).reshape(nb, rows_i, k_blk).sum(axis=2)
                for index_edge in range(NEDGE)
            ],
            axis=-1,
        )
        energy_slot = jnp.zeros((nb, rows_i, depth_k), jnp.float32)
        energy_slot = lax.dynamic_update_slice_in_dim(energy_slot, energy_part, g * k_blk, axis=2)
        packed = all_reduce(jnp.concatenate([energy_slot, ramp_part], axis=2), "group", n_group)
        energy = packed[:, :, :depth_k]
        ramp_sums = packed[:, :, depth_k:]
        histogram = (ramp_sums[..., :-1] - ramp_sums[..., 1:]) * (NBINS / (n2 * depth_k))
        return (basis_one, basis_two, core_block, residual_block, energy, histogram)

    return local


def solution(mesh):
    in_specs = (P("inner", "group", None), P("inner", None), P("group", None), P(), P(), P())
    out_specs = (
        P("inner", None),
        P("group", None),
        P("inner", "group", None),
        P(None, "inner", "group", None),
        P(None, "inner", None),
        P(None, "inner", None),
    )
    local = make_local(mesh.shape["group"], mesh.shape["inner"])
    return jax.shard_map(local, mesh=mesh, in_specs=in_specs, out_specs=out_specs, check_vma=False)
```

time: 864 us -> 350 us (0.41)
  waiting for transfers between devices: 571 us -> 99.8 us
  blocking collectives: 142 us -> 0 us
  starting transfers between devices: 0.61 us -> 118 us
  matrix products: 74.1 us -> 59.7 us
    reduce_scatter x2 -> x0, waiting for transfers between devices: 227 us -> none  [the longest x1 214 us: local(): lax.psum_scatter(partial_rows, 'inner', scatter_dimension=0, tiled=True)]
    psum x2 -> x0, waiting for transfers between devices: 209 us -> none  [the longest x1 144 us: local(): basis_one = orthonormal_rows(mode_one, lax.psum(gram_of(mode_one), 'inner'))]
    all_gather x1 -> x0, waiting for transfers between devices: 135 us -> none  [local(): lax.all_gather(spread, 'inner', axis=1, tiled=True)]
    ppermute x0 -> x46, starting transfers between devices: none -> 118 us  [the longest x27 72.7 us: all_reduce(): x = op(x, lax.ppermute(x, axis, xor_pairs(n, d)))]
    ppermute x0 -> x46, waiting for transfers between devices: none -> 99.8 us  [the longest x27 65 us: all_reduce(): x = op(x, lax.ppermute(x, axis, xor_pairs(n, d)))]
    pmax x1 -> x0, blocking collectives: 79.6 us -> none  [local(): peak = lax.pmax(jnp.max(jnp.abs(core_shard)), ('group', 'inner'))]
    psum x2 -> x0, blocking collectives: 47.8 us -> none  [the longest x1 24 us: local(): mode_one = lax.psum(mode_one, 'group')]
    all_gather x1 -> x0, blocking collectives: 14.9 us -> none  [local(): spread = lax.all_gather(residual_shard, 'group', axis=2, tiled=True)]
  transfers between devices with their start and end apart: 5 -> 46, of which waited for: 5 -> 35; matrix products, arithmetic and copies ran while one was open for 3% -> 20% of each run, Pallas kernels for 0% -> 0%
where the time goes in v1:
time: 350 us; the launch traced here: 344 us
  starting transfers between devices  118 us (34%)
  waiting for transfers between devices  99.8 us (29%)
  matrix products  59.7 us (17%)
  other arithmetic  52.6 us (15%)
  between operations  6.98 us (2%)
  local copies, waits for them, and re-layouts  6.45 us (2%)
    ppermute x27, starting transfers between devices, all_reduce(): x = op(x, lax.ppermute(x, axis, xor_pairs(n, d)))  72.7 us
    ppermute x27, waiting for transfers between devices, all_reduce(): x = op(x, lax.ppermute(x, axis, xor_pairs(n, d)))  65 us
    ppermute x11, starting transfers between devices, all_gather(): other = lax.ppermute(x, axis, xor_pairs(n, d))  28.1 us
    dot_general x1, matrix products, local(): field_error = error_scale * jnp.dot(basis_two_all, mixed, precision=precise)  27.9 us
    another operation x6, other arithmetic, orthonormal_rows(): lower_factor = jnp.linalg.cholesky(gram_matrix)  24.8 us
    another operation x4, other arithmetic, orthonormal_rows(): jax.scipy.linalg.solve_triangular(lower_factor, sketch.T, lower=True)  20.9 us
    ppermute x8, waiting for transfers between devices, reduce_scatter(): x = keep + lax.ppermute(send, axis, xor_pairs(n, d))  20.7 us
    ppermute x8, starting transfers between devices, reduce_scatter(): x = keep + lax.ppermute(send, axis, xor_pairs(n, d))  17.5 us
  transfers between devices with their start and end apart: 46, of which 35 were waited for; matrix products, arithmetic and copies ran while one was open for 20% of the time, Pallas kernels for 0%

profile of v1, /device:TPU:1, one launch (start us, length us, event | category | flops | bytes accessed | tf_op | source)
XLA Modules:
  0.0 343.9 jit_solution(7664590761755685197)
XLA Ops:
  1.5 6.0 %multiply_reduce_fusion.2 = (f32[128,48]{0,1:T(8,128)S(1)}, f32[48,192,128]{2,1,0:T(8,128)S(1)}) fusion(f32[128,192]{0,1:T(8,128)} %bitcast.238, f32[48,192,128]{2,1,0:T(8,128)} %param.7, f32[128,128]{1,0:T(8,128)S(1)} %copy-done), kind=kOutput, calls=%fused_computation.12 | convolution fusion | flops 1814292480 | bytes 9625600 | tf_op jit(solution)/shard_map/ijk,kr->ijr/dot_general | solution.py:91
  8.1 2.2 collective-permute-start.8
  10.3 2.4 collective-permute-done.8
  12.7 3.7 %collective-permute-start.9 = (f32[192,128]{0,1:T(8,128)S(1)}, f32[192,128]{0,1:T(8,128)S(1)}, u32[]{:S(2)}, u32[]{:S(2)}) collective-permute-start(f32[192,128]{0,1:T(8,128)S(1)} %bitcast_add_fusion.11), channel_id=1, source_target_pairs={{0,2},{1,3},{2,0},{3,1},{4,6},{5,7},{6,4},{7,5},{8,10},{9,11},{10,... | collective-permute-start | bytes 294920 | tf_op jit(solution)/shard_map/ppermute | solution.py:41
  16.4 2.4 collective-permute-done.9
  18.8 1.8 collective-permute-start.10
  20.6 2.4 collective-permute-done.10
  23.0 3.1 collective-permute-start.11
  26.0 2.7 collective-permute-done.11
  28.7 7.3 %collective-permute-start.12 = (f32[192,128]{0,1:T(8,128)S(1)}, f32[192,128]{0,1:T(8,128)S(1)}, u32[]{:S(2)}, u32[]{:S(2)}) collective-permute-start(f32[192,128]{0,1:T(8,128)S(1)} %add.249), channel_id=1, source_target_pairs={{0,16},{1,17},{2,18},{3,19},{4,20},{5,21},{6,22},{7,23},{8,24},{9,... | collective-permute-start | bytes 294920 | tf_op jit(solution)/shard_map/ppermute | solution.py:41
  36.0 3.3 collective-permute-done.12
  39.6 6.4 %collective-permute-start.13 = (f32[128,128]{0,1:T(8,128)S(1)}, f32[128,128]{0,1:T(8,128)S(1)}, u32[]{:S(2)}, u32[]{:S(2)}) collective-permute-start(f32[128,128]{0,1:T(8,128)S(1)} %fusion.33), channel_id=1, source_target_pairs={{0,32},{32,0},{64,96},{96,64},{128,160},{160,128},{192,224},{224,1... | collective-permute-start | bytes 196616 | tf_op jit(solution)/shard_map/ppermute | solution.py:41
  48.2 1.9 collective-permute-done.14
  50.1 3.3 collective-permute-start.15
  53.4 1.9 collective-permute-done.15
  55.4 11.7 %cholesky.55 = f32[128,128]{1,0:T(8,128)S(1)} custom-call(f32[128,128]{1,0:T(8,128)S(1)} %fusion.20), custom_call_target="Cholesky" | custom-call | tf_op jit(solution)/shard_map/jit(cholesky)/cholesky | solution.py:22
  68.5 9.8 %custom-call.11 = f32[1,128,128]{1,2,0:T(8,128)S(1)} custom-call(f32[1,128,128]{2,1,0:T(8,128)S(1)} %fusion.17), custom_call_target="InvertDiagBlocksLowerTriangular" | custom-call | tf_op jit(solution)/shard_map/jit(_solve_triangular)/triangular_solve | solution.py:23
  78.7 11.9 %fusion.12 = f32[128,48,128]{0,2,1:T(8,128)S(1)} fusion(f32[48,192,128]{2,1,0:T(8,128)} %param.7, f32[128,192]{0,1:T(8,128)S(1)} %fusion.18), kind=kOutput, calls=%fused_computation.55 | convolution fusion | flops 1811939328 | bytes 7962624 | tf_op jit(solution)/shard_map/ijk,js->kis/dot_general | solution.py:100
  92.0 2.8 collective-permute-start.16
  95.0 3.2 collective-permute-done
  99.5 1.9 collective-permute-done.1
  101.4 2.8 collective-permute-start.2
  104.2 1.9 collective-permute-done.2
  106.1 1.8 bitcast_add_fusion
  111.5 1.8 collective-permute-done.3
  113.4 3.0 collective-permute-start.4
  116.4 1.7 collective-permute-done.4
  118.2 3.4 collective-permute-done.5
  122.2 4.0 %collective-permute-done.6 = f32[128,128]{0,1:T(8,128)S(1)} collective-permute-done((f32[128,128]{0,1:T(8,128)S(1)}, f32[128,128]{0,1:T(8,128)S(1)}, u32[]{:S(2)}, u32[]{:S(2)}) %collective-permute-start.6) | collective-permute-done | bytes 65568 | tf_op jit(solution)/shard_map/ppermute | solution.py:41
  126.1 5.7 %collective-permute-start.7 = (f32[128,128]{0,1:T(8,128)S(1)}, f32[128,128]{0,1:T(8,128)S(1)}, u32[]{:S(2)}, u32[]{:S(2)}) collective-permute-start(f32[128,128]{0,1:T(8,128)S(1)} %add.244), channel_id=1, source_target_pairs={{0,16},{1,17},{2,18},{3,19},{4,20},{5,21},{6,22},{7,23},{8,24},{9,... | collective-permute-start | bytes 196616 | tf_op jit(solution)/shard_map/ppermute | solution.py:41
  131.9 1.7 collective-permute-done.7
  133.7 11.7 %cholesky.44 = f32[128,128]{1,0:T(8,128)S(1)} custom-call(f32[128,128]{1,0:T(8,128)S(1)} %fusion.23), custom_call_target="Cholesky" | custom-call | tf_op jit(solution)/shard_map/jit(cholesky)/cholesky | solution.py:22
  146.6 2.7 collective-permute-start.18
  150.0 9.8 %custom-call.10 = f32[1,128,128]{1,2,0:T(8,128)S(1)} custom-call(f32[1,128,128]{2,1,0:T(8,128)S(1)} %fusion.16), custom_call_target="InvertDiagBlocksLowerTriangular" | custom-call | tf_op jit(solution)/shard_map/jit(_solve_triangular)/triangular_solve | solution.py:23
  161.2 1.7 collective-permute-start.19
  162.9 6.6 %collective-permute-done.19 = f32[2,2,2,2,64,128]{5,4,3,2,1,0:T(8,128)S(1)} collective-permute-done((f32[2,2,2,2,64,128]{5,4,3,2,1,0:T(8,128)S(1)}, f32[2,2,2,2,64,128]{5,4,3,2,1,0:T(8,128)S(1)}, u32[]{:S(2)}, u32[]{:S(2)}) %collective-permute-start.19) | collective-permute-done | bytes 524320 | tf_op jit(solution)/shard_map/ppermute | solution.py:57
  169.6 2.8 collective-permute-start.20
  172.9 5.6 %collective-permute-done.20 = f32[2,2,2,64,128]{4,3,2,1,0:T(8,128)S(1)} collective-permute-done((f32[2,2,2,64,128]{4,3,2,1,0:T(8,128)S(1)}, f32[2,2,2,64,128]{4,3,2,1,0:T(8,128)S(1)}, u32[]{:S(2)}, u32[]{:S(2)}) %collective-permute-start.20) | collective-permute-done | bytes 262176 | tf_op jit(solution)/shard_map/ppermute | solution.py:57
  179.4 3.1 collective-permute-done.21
  183.1 4.3 %collective-permute-done.22 = f32[2,64,128]{2,1,0:T(8,128)S(1)} collective-permute-done((f32[2,64,128]{2,1,0:T(8,128)S(1)}, f32[2,64,128]{2,1,0:T(8,128)S(1)}, u32[]{:S(2)}, u32[]{:S(2)}) %collective-permute-start.22) | collective-permute-done | bytes 65568 | tf_op jit(solution)/shard_map/ppermute | solution.py:57
  187.4 5.4 %collective-permute-start.23 = (f32[64,128]{1,0:T(8,128)S(1)}, f32[64,128]{1,0:T(8,128)S(1)}, u32[]{:S(2)}, u32[]{:S(2)}) collective-permute-start(f32[64,128]{1,0:T(8,128)S(1)} %dynamic-slice_bitcast_fusion.6), channel_id=1, source_target_pairs={{0,16},{1,17},{2,18},{3,19},{4,20},{5,21},{6,22},{7,23},{8,24},{9,... | collective-permute-start | bytes 98312 | tf_op jit(solution)/shard_map/ppermute | solution.py:57
  194.8 5.4 %collective-permute-start.24 = (f32[64,128]{1,0:T(8,128)S(1)}, f32[64,128]{1,0:T(8,128)S(1)}, u32[]{:S(2)}, u32[]{:S(2)}) collective-permute-start(f32[64,128]{1,0:T(8,128)S(1)} %get-tuple-element.48), channel_id=1, source_target_pairs={{0,16},{1,17},{2,18},{3,19},{4,20},{5,21},{6,22},{7,23},{8,24},{9,... | collective-permute-start | bytes 98312 | tf_op jit(solution)/shard_map/ppermute | solution.py:71
  200.2 15.3 %collective-permute-start.42 = (f32[2,2,192,128]{3,2,0,1:T(8,128)S(1)}, f32[2,2,192,128]{3,2,0,1:T(8,128)S(1)}, u32[]{:S(2)}, u32[]{:S(2)}) collective-permute-start(f32[2,2,192,128]{3,2,0,1:T(8,128)S(1)} %maximum_select_fusion.5), channel_id=1, source_target_pairs={{0,32},{32,0},{64,96},{96,64},{128,160},{160,128},{192,224},{224,1... | collective-permute-start | bytes 1179656 | tf_op jit(solution)/shard_map/ppermute | solution.py:71
  215.7 4.2 %collective-permute-done.25 = f32[2,64,128]{2,1,0:T(8,128)S(1)} collective-permute-done((f32[2,64,128]{2,1,0:T(8,128)S(1)}, f32[2,64,128]{2,1,0:T(8,128)S(1)}, u32[]{:S(2)}, u32[]{:S(2)}) %collective-permute-start.25) | collective-permute-done | bytes 65568 | tf_op jit(solution)/shard_map/ppermute | solution.py:71
  220.0 3.8 %collective-permute-done.26 = f32[2,2,64,128]{3,2,0,1:T(8,128)S(1)} collective-permute-done((f32[2,2,64,128]{3,2,0,1:T(8,128)S(1)}, f32[2,2,64,128]{3,2,0,1:T(8,128)S(1)}, u32[]{:S(2)}, u32[]{:S(2)}) %collective-permute-start.26) | collective-permute-done | bytes 131104 | tf_op jit(solution)/shard_map/ppermute | solution.py:71
  223.8 2.7 collective-permute-start.27
  226.5 4.1 %collective-permute-done.27 = f32[2,2,2,64,128]{4,3,0,2,1:T(8,128)S(1)} collective-permute-done((f32[2,2,2,64,128]{4,3,0,2,1:T(8,128)S(1)}, f32[2,2,2,64,128]{4,3,0,2,1:T(8,128)S(1)}, u32[]{:S(2)}, u32[]{:S(2)}) %collective-permute-start.27) | collective-permute-done | bytes 262176 | tf_op jit(solution)/shard_map/ppermute | solution.py:71
  230.7 1.6 collective-permute-start.28
  232.5 8.1 %collective-permute-done.32 = f32[]{:T(128)} collective-permute-done((f32[]{:T(128)}, f32[]{:T(128)}, u32[]{:S(2)}, u32[]{:S(2)}) %collective-permute-start.32) | collective-permute-done | bytes 36 | tf_op jit(solution)/shard_map/ppermute | solution.py:41
  241.8 3.3 collective-permute-start.33
  247.4 1.6 collective-permute-done.34
  250.9 2.1 collective-permute-done.35
  253.6 1.6 collective-permute-start.36
  255.2 4.8 %collective-permute-done.36 = f32[]{:T(128)} collective-permute-done((f32[]{:T(128)}, f32[]{:T(128)}, u32[]{:S(2)}, u32[]{:S(2)}) %collective-permute-start.36) | collective-permute-done | bytes 36 | tf_op jit(solution)/shard_map/ppermute | solution.py:41
  260.5 12.8 %collective-permute-start.37 = (f32[]{:T(128)}, f32[]{:T(128)}, u32[]{:S(2)}, u32[]{:S(2)}) collective-permute-start(f32[]{:T(128)} %max.50), channel_id=1, source_target_pairs={{0,32},{32,0},{64,96},{96,64},{128,160},{160,128},{192,224},{224,1... | collective-permute-start | bytes 20 | tf_op jit(solution)/shard_map/ppermute | solution.py:41
  274.7 1.6 collective-permute-done.38
  278.3 2.6 collective-permute-done.39
  282.6 11.7 %fusion.4 = f32[128,2,48,16]{0,2,3,1:T(8,128)S(1)} fusion(f32[2]{0:T(128)S(1)} %add_divide_fusion, f32[16,128,128]{2,1,0:T(8,128)S(1)} %broadcast_multiply_fusion, f32[128,48]{0,1:T(8,128)S(1)} %fusion.21), kind=kOutput, calls=%fused_computation.19 | convolution fusion | flops 303562752 | bytes 1859592 | tf_op jit(solution)/shard_map/ir,bkrs->sbik/dot_general | solution.py:119
  294.6 27.9 %clamp_reduce_fusion = (f32[1536]{0:T(1024)S(1)}, f32[1536]{0:T(1024)S(1)}, f32[1536]{0:T(1024)S(1)}, f32[1536]{0:T(1024)S(1)}, f32[1536]{0:T(1024)S(1)}, /*inde...) fusion(f32[]{:T(128)} %bitcast.104, f32[]{:T(128)} %bitcast.101, ...), kind=kOutput, calls=%fused_computation.1 | convolution fusion | flops 3715875840 | bytes 1634340 | tf_op jit(solution)/shard_map/dot_general | solution.py:123
  324.4 3.3 collective-permute-start.43
  329.4 2.0 collective-permute-done.30
  332.8 1.8 collective-permute-done.44
  334.7 2.5 collective-permute-start.45
  337.2 3.6 %collective-permute-done.45 = f32[2,48,137]{1,2,0:T(8,128)S(1)} collective-permute-done((f32[2,48,137]{1,2,0:T(8,128)S(1)}, f32[2,48,137]{1,2,0:T(8,128)S(1)}, u32[]{:S(2)}, u32[]{:S(2)}) %collective-permute-start.45) | collective-permute-done | bytes 52640 | tf_op jit(solution)/shard_map/ppermute | solution.py:41
  (167 shorter events, 35.0 us)
Async XLA Ops:
  0.6 0.8 copy-start
  1.5 6.0 %copy-start.4 = (f32[48,128]{1,0:T(8,128)S(1)}, f32[48,128]{1,0:T(8,128)}, u32[]{:S(2)}) copy-start(f32[48,128]{1,0:T(8,128)} %param.8) | copy-start | bytes 73732
  8.1 4.6 %collective-permute-start.8 = (f32[192,128]{0,1:T(8,128)S(1)}, f32[192,128]{0,1:T(8,128)S(1)}, u32[]{:S(2)}, u32[]{:S(2)}) collective-permute-start(f32[192,128]{0,1:T(8,128)S(1)} %bitcast.220), channel_id=1, source_target_pairs={{0,1},{1,0},{2,3},{3,2},{4,5},{5,4},{6,7},{7,6},{8,9},{9,8},{10,11... | collective-permute-start | bytes 294920 | tf_op jit(solution)/shard_map/ppermute | solution.py:41
  12.7 6.1 %collective-permute-start.9 = (f32[192,128]{0,1:T(8,128)S(1)}, f32[192,128]{0,1:T(8,128)S(1)}, u32[]{:S(2)}, u32[]{:S(2)}) collective-permute-start(f32[192,128]{0,1:T(8,128)S(1)} %bitcast_add_fusion.11), channel_id=1, source_target_pairs={{0,2},{1,3},{2,0},{3,1},{4,6},{5,7},{6,4},{7,5},{8,10},{9,11},{10,... | collective-permute-start | bytes 294920 | tf_op jit(solution)/shard_map/ppermute | solution.py:41
  18.8 4.1 %collective-permute-start.10 = (f32[192,128]{0,1:T(8,128)S(1)}, f32[192,128]{0,1:T(8,128)S(1)}, u32[]{:S(2)}, u32[]{:S(2)}) collective-permute-start(f32[192,128]{0,1:T(8,128)S(1)} %add.247), channel_id=1, source_target_pairs={{0,4},{1,5},{2,6},{3,7},{4,0},{5,1},{6,2},{7,3},{8,12},{9,13},{10,... | collective-permute-start | bytes 294920 | tf_op jit(solution)/shard_map/ppermute | solution.py:41
  23.0 5.8 %collective-permute-start.11 = (f32[192,128]{0,1:T(8,128)S(1)}, f32[192,128]{0,1:T(8,128)S(1)}, u32[]{:S(2)}, u32[]{:S(2)}) collective-permute-start(f32[192,128]{0,1:T(8,128)S(1)} %add.248), channel_id=1, source_target_pairs={{0,8},{1,9},{2,10},{3,11},{4,12},{5,13},{6,14},{7,15},{8,0},{9,1},... | collective-permute-start | bytes 294920 | tf_op jit(solution)/shard_map/ppermute | solution.py:41
  28.7 10.6 %collective-permute-start.12 = (f32[192,128]{0,1:T(8,128)S(1)}, f32[192,128]{0,1:T(8,128)S(1)}, u32[]{:S(2)}, u32[]{:S(2)}) collective-permute-start(f32[192,128]{0,1:T(8,128)S(1)} %add.249), channel_id=1, source_target_pairs={{0,16},{1,17},{2,18},{3,19},{4,20},{5,21},{6,22},{7,23},{8,24},{9,... | collective-permute-start | bytes 294920 | tf_op jit(solution)/shard_map/ppermute | solution.py:41
  39.6 7.3 %collective-permute-start.13 = (f32[128,128]{0,1:T(8,128)S(1)}, f32[128,128]{0,1:T(8,128)S(1)}, u32[]{:S(2)}, u32[]{:S(2)}) collective-permute-start(f32[128,128]{0,1:T(8,128)S(1)} %fusion.33), channel_id=1, source_target_pairs={{0,32},{32,0},{64,96},{96,64},{128,160},{160,128},{192,224},{224,1... | collective-permute-start | bytes 196616 | tf_op jit(solution)/shard_map/ppermute | solution.py:41
  46.9 3.2 collective-permute-start.14
  50.1 5.2 %collective-permute-start.15 = (f32[128,128]{0,1:T(8,128)S(1)}, f32[128,128]{0,1:T(8,128)S(1)}, u32[]{:S(2)}, u32[]{:S(2)}) collective-permute-start(f32[128,128]{0,1:T(8,128)S(1)} %add.252), channel_id=1, source_target_pairs={{0,128},{32,160},{64,192},{96,224},{128,0},{160,32},{192,64},{224,... | collective-permute-start | bytes 196616 | tf_op jit(solution)/shard_map/ppermute | solution.py:41
  78.7 114.2 %copy-start.1 = (f32[128,192]{0,1:T(8,128)}, f32[128,192]{0,1:T(8,128)S(1)}, u32[]{:S(2)}) copy-start(f32[128,192]{0,1:T(8,128)S(1)} %fusion.18) | copy-start | bytes 294916
  92.0 14.1 %collective-permute-start.16 = (f32[2,2,16,48,128]{4,2,1,0,3:T(8,128)}, f32[2,2,16,48,128]{4,2,1,0,3:T(8,128)}, u32[]{:S(2)}, u32[]{:S(2)}) collective-permute-start(f32[2,2,16,48,128]{4,2,1,0,3:T(8,128)} %dynamic-slice_bitcast_fusion), channel_id=1, source_target_pairs={{0,32},{32,0},{64,96},{96,64},{128,160},{160,128},{192,224},{224,1... | collective-permute-start | bytes 4718600 | tf_op jit(solution)/shard_map/ppermute | solution.py:57
  94.9 3.3 collective-permute-start
  98.2 3.2 collective-permute-start.1
  101.4 4.7 %collective-permute-start.2 = (f32[48,128]{0,1:T(8,128)S(1)}, f32[48,128]{0,1:T(8,128)S(1)}, u32[]{:S(2)}, u32[]{:S(2)}) collective-permute-start(f32[48,128]{0,1:T(8,128)S(1)} %add.239), channel_id=1, source_target_pairs={{0,128},{32,160},{64,192},{96,224},{128,0},{160,32},{192,64},{224,... | collective-permute-start | bytes 73736 | tf_op jit(solution)/shard_map/ppermute | solution.py:41
  108.6 37.5 %collective-permute-start.17 = (f32[2,16,48,128]{3,2,1,0:T(8,128)S(1)}, f32[2,16,48,128]{3,2,1,0:T(8,128)S(1)}, u32[]{:S(2)}, u32[]{:S(2)}) collective-permute-start(f32[2,16,48,128]{3,2,1,0:T(8,128)S(1)} %bitcast.213), channel_id=1, source_target_pairs={{0,64},{32,96},{64,0},{96,32},{128,192},{160,224},{192,128},{224,1... | collective-permute-start | bytes 2359304 | tf_op jit(solution)/shard_map/ppermute | solution.py:57
  110.1 3.2 collective-permute-start.3
  113.4 4.7 %collective-permute-start.4 = (f32[128,128]{0,1:T(8,128)S(1)}, f32[128,128]{0,1:T(8,128)S(1)}, u32[]{:S(2)}, u32[]{:S(2)}) collective-permute-start(f32[128,128]{0,1:T(8,128)S(1)} %add.241), channel_id=1, source_target_pairs={{0,2},{1,3},{2,0},{3,1},{4,6},{5,7},{6,4},{7,5},{8,10},{9,11},{10,... | collective-permute-start | bytes 196616 | tf_op jit(solution)/shard_map/ppermute | solution.py:41
  118.1 3.5 %collective-permute-start.5 = (f32[128,128]{0,1:T(8,128)S(1)}, f32[128,128]{0,1:T(8,128)S(1)}, u32[]{:S(2)}, u32[]{:S(2)}) collective-permute-start(f32[128,128]{0,1:T(8,128)S(1)} %add.242), channel_id=1, source_target_pairs={{0,4},{1,5},{2,6},{3,7},{4,0},{5,1},{6,2},{7,3},{8,12},{9,13},{10,... | collective-permute-start | bytes 196616 | tf_op jit(solution)/shard_map/ppermute | solution.py:41
  121.6 50.8 %copy-start.5 = (s32[9]{0:T(128)S(1)}, s32[9]{0:T(128)}, u32[]{:S(2)}) copy-start(s32[9]{0:T(128)} %param.12) | copy-start | bytes 112
  121.6 4.5 %collective-permute-start.6 = (f32[128,128]{0,1:T(8,128)S(1)}, f32[128,128]{0,1:T(8,128)S(1)}, u32[]{:S(2)}, u32[]{:S(2)}) collective-permute-start(f32[128,128]{0,1:T(8,128)S(1)} %add.243), channel_id=1, source_target_pairs={{0,8},{1,9},{2,10},{3,11},{4,12},{5,13},{6,14},{7,15},{8,0},{9,1},... | collective-permute-start | bytes 196616 | tf_op jit(solution)/shard_map/ppermute | solution.py:41
  126.1 7.4 %collective-permute-start.7 = (f32[128,128]{0,1:T(8,128)S(1)}, f32[128,128]{0,1:T(8,128)S(1)}, u32[]{:S(2)}, u32[]{:S(2)}) collective-permute-start(f32[128,128]{0,1:T(8,128)S(1)} %add.244), channel_id=1, source_target_pairs={{0,16},{1,17},{2,18},{3,19},{4,20},{5,21},{6,22},{7,23},{8,24},{9,... | collective-permute-start | bytes 196616 | tf_op jit(solution)/shard_map/ppermute | solution.py:41
  146.6 13.5 %collective-permute-start.18 = (f32[16,48,128]{2,1,0:T(8,128)S(1)}, f32[16,48,128]{2,1,0:T(8,128)S(1)}, u32[]{:S(2)}, u32[]{:S(2)}) collective-permute-start(f32[16,48,128]{2,1,0:T(8,128)S(1)} %dynamic-slice_bitcast_fusion.2), channel_id=1, source_target_pairs={{0,128},{32,160},{64,192},{96,224},{128,0},{160,32},{192,64},{224,... | collective-permute-start | bytes 1179656 | tf_op jit(solution)/shard_map/ppermute | solution.py:57
  160.1 122.5 %copy-start.3 = (f32[128,48]{0,1:T(8,128)}, f32[128,48]{0,1:T(8,128)S(1)}, u32[]{:S(2)}) copy-start(f32[128,48]{0,1:T(8,128)S(1)} %fusion.21) | copy-start | bytes 73732
  161.2 8.3 %collective-permute-start.19 = (f32[2,2,2,2,64,128]{5,4,3,2,1,0:T(8,128)S(1)}, f32[2,2,2,2,64,128]{5,4,3,2,1,0:T(8,128)S(1)}, u32[]{:S(2)}, u32[]{:S(2)}) collective-permute-start(f32[2,2,2,2,64,128]{5,4,3,2,1,0:T(8,128)S(1)} %dynamic-slice_bitcast_fusion.1), channel_id=1, source_target_pairs={{0,1},{1,0},{2,3},{3,2},{4,5},{5,4},{6,7},{7,6},{8,9},{9,8},{10,11... | collective-permute-start | bytes 1572872 | tf_op jit(solution)/shard_map/ppermute | solution.py:57
  169.6 9.0 %collective-permute-start.20 = (f32[2,2,2,64,128]{4,3,2,1,0:T(8,128)S(1)}, f32[2,2,2,64,128]{4,3,2,1,0:T(8,128)S(1)}, u32[]{:S(2)}, u32[]{:S(2)}) collective-permute-start(f32[2,2,2,64,128]{4,3,2,1,0:T(8,128)S(1)} %dynamic-slice_bitcast_fusion.3), channel_id=1, source_target_pairs={{0,2},{1,3},{2,0},{3,1},{4,6},{5,7},{6,4},{7,5},{8,10},{9,11},{10,... | collective-permute-start | bytes 786440 | tf_op jit(solution)/shard_map/ppermute | solution.py:57
  172.4 7.0 %collective-permute-start.40 = (f32[192,128]{1,0:T(8,128)S(1)}, f32[192,128]{1,0:T(8,128)S(1)}, u32[]{:S(2)}, u32[]{:S(2)}) collective-permute-start(f32[192,128]{1,0:T(8,128)S(1)} %bitcast.203), channel_id=1, source_target_pairs={{0,128},{32,160},{64,192},{96,224},{128,0},{160,32},{192,64},{224,... | collective-permute-start | bytes 294920 | tf_op jit(solution)/shard_map/ppermute | solution.py:71
  178.6 3.9 %collective-permute-start.21 = (f32[2,2,64,128]{3,2,1,0:T(8,128)S(1)}, f32[2,2,64,128]{3,2,1,0:T(8,128)S(1)}, u32[]{:S(2)}, u32[]{:S(2)}) collective-permute-start(f32[2,2,64,128]{3,2,1,0:T(8,128)S(1)} %dynamic-slice_bitcast_fusion.4), channel_id=1, source_target_pairs={{0,4},{1,5},{2,6},{3,7},{4,0},{5,1},{6,2},{7,3},{8,12},{9,13},{10,... | collective-permute-start | bytes 393224 | tf_op jit(solution)/shard_map/ppermute | solution.py:57
  179.4 102.0 %copy-start.6 = (s32[2]{0:T(128)S(1)}, s32[2]{0:T(128)}, u32[]{:S(2)}) copy-start(s32[2]{0:T(128)} %param.11) | copy-start | bytes 28
  182.5 4.8 %collective-permute-start.22 = (f32[2,64,128]{2,1,0:T(8,128)S(1)}, f32[2,64,128]{2,1,0:T(8,128)S(1)}, u32[]{:S(2)}, u32[]{:S(2)}) collective-permute-start(f32[2,64,128]{2,1,0:T(8,128)S(1)} %dynamic-slice_bitcast_fusion.5), channel_id=1, source_target_pairs={{0,8},{1,9},{2,10},{3,11},{4,12},{5,13},{6,14},{7,15},{8,0},{9,1},... | collective-permute-start | bytes 196616 | tf_op jit(solution)/shard_map/ppermute | solution.py:57
  187.4 6.8 %collective-permute-start.23 = (f32[64,128]{1,0:T(8,128)S(1)}, f32[64,128]{1,0:T(8,128)S(1)}, u32[]{:S(2)}, u32[]{:S(2)}) collective-permute-start(f32[64,128]{1,0:T(8,128)S(1)} %dynamic-slice_bitcast_fusion.6), channel_id=1, source_target_pairs={{0,16},{1,17},{2,18},{3,19},{4,20},{5,21},{6,22},{7,23},{8,24},{9,... | collective-permute-start | bytes 98312 | tf_op jit(solution)/shard_map/ppermute | solution.py:57
  192.9 7.3 %collective-permute-start.41 = (f32[2,192,128]{2,1,0:T(8,128)S(1)}, f32[2,192,128]{2,1,0:T(8,128)S(1)}, u32[]{:S(2)}, u32[]{:S(2)}) collective-permute-start(f32[2,192,128]{2,1,0:T(8,128)S(1)} %maximum_select_fusion.10), channel_id=1, source_target_pairs={{0,64},{32,96},{64,0},{96,32},{128,192},{160,224},{192,128},{224,1... | collective-permute-start | bytes 589832 | tf_op jit(solution)/shard_map/ppermute | solution.py:71
  194.8 20.7 %collective-permute-start.24 = (f32[64,128]{1,0:T(8,128)S(1)}, f32[64,128]{1,0:T(8,128)S(1)}, u32[]{:S(2)}, u32[]{:S(2)}) collective-permute-start(f32[64,128]{1,0:T(8,128)S(1)} %get-tuple-element.48), channel_id=1, source_target_pairs={{0,16},{1,17},{2,18},{3,19},{4,20},{5,21},{6,22},{7,23},{8,24},{9,... | collective-permute-start | bytes 98312 | tf_op jit(solution)/shard_map/ppermute | solution.py:71
  200.2 32.1 %collective-permute-start.42 = (f32[2,2,192,128]{3,2,0,1:T(8,128)S(1)}, f32[2,2,192,128]{3,2,0,1:T(8,128)S(1)}, u32[]{:S(2)}, u32[]{:S(2)}) collective-permute-start(f32[2,2,192,128]{3,2,0,1:T(8,128)S(1)} %maximum_select_fusion.5), channel_id=1, source_target_pairs={{0,32},{32,0},{64,96},{96,64},{128,160},{160,128},{192,224},{224,1... | collective-permute-start | bytes 1179656 | tf_op jit(solution)/shard_map/ppermute | solution.py:71
  215.5 4.4 %collective-permute-start.25 = (f32[2,64,128]{2,1,0:T(8,128)S(1)}, f32[2,64,128]{2,1,0:T(8,128)S(1)}, u32[]{:S(2)}, u32[]{:S(2)}) collective-permute-start(f32[2,64,128]{2,1,0:T(8,128)S(1)} %maximum_select_fusion.16), channel_id=1, source_target_pairs={{0,8},{1,9},{2,10},{3,11},{4,12},{5,13},{6,14},{7,15},{8,0},{9,1},... | collective-permute-start | bytes 196616 | tf_op jit(solution)/shard_map/ppermute | solution.py:71
  219.9 3.9 %collective-permute-start.26 = (f32[2,2,64,128]{3,2,0,1:T(8,128)S(1)}, f32[2,2,64,128]{3,2,0,1:T(8,128)S(1)}, u32[]{:S(2)}, u32[]{:S(2)}) collective-permute-start(f32[2,2,64,128]{3,2,0,1:T(8,128)S(1)} %maximum_select_fusion.12), channel_id=1, source_target_pairs={{0,4},{1,5},{2,6},{3,7},{4,0},{5,1},{6,2},{7,3},{8,12},{9,13},{10,... | collective-permute-start | bytes 393224 | tf_op jit(solution)/shard_map/ppermute | solution.py:71
  223.8 6.8 %collective-permute-start.27 = (f32[2,2,2,64,128]{4,3,0,2,1:T(8,128)S(1)}, f32[2,2,2,64,128]{4,3,0,2,1:T(8,128)S(1)}, u32[]{:S(2)}, u32[]{:S(2)}) collective-permute-start(f32[2,2,2,64,128]{4,3,0,2,1:T(8,128)S(1)} %maximum_select_fusion.7), channel_id=1, source_target_pairs={{0,2},{1,3},{2,0},{3,1},{4,6},{5,7},{6,4},{7,5},{8,10},{9,11},{10,... | collective-permute-start | bytes 786440 | tf_op jit(solution)/shard_map/ppermute | solution.py:71
  230.7 50.8 %collective-permute-start.28 = (f32[2,2,2,2,64,128]{5,4,0,2,1,3:T(8,128)S(1)}, f32[2,2,2,2,64,128]{5,4,0,2,1,3:T(8,128)S(1)}, u32[]{:S(2)}, u32[]{:S(2)}) collective-permute-start(f32[2,2,2,2,64,128]{5,4,0,2,1,3:T(8,128)S(1)} %maximum_select_fusion.3), channel_id=1, source_target_pairs={{0,1},{1,0},{2,3},{3,2},{4,5},{5,4},{6,7},{7,6},{8,9},{9,8},{10,11... | collective-permute-start | bytes 1572872 | tf_op jit(solution)/shard_map/ppermute | solution.py:71
  232.4 8.2 %collective-permute-start.32 = (f32[]{:T(128)}, f32[]{:T(128)}, u32[]{:S(2)}, u32[]{:S(2)}) collective-permute-start(f32[]{:T(128)} %get-tuple-element.47), channel_id=1, source_target_pairs={{0,1},{1,0},{2,3},{3,2},{4,5},{5,4},{6,7},{7,6},{8,9},{9,8},{10,11... | collective-permute-start | bytes 20 | tf_op jit(solution)/shard_map/ppermute | solution.py:41
  241.8 4.2 %collective-permute-start.33 = (f32[]{:T(128)}, f32[]{:T(128)}, u32[]{:S(2)}, u32[]{:S(2)}) collective-permute-start(f32[]{:T(128)} %max.46), channel_id=1, source_target_pairs={{0,2},{1,3},{2,0},{3,1},{4,6},{5,7},{6,4},{7,5},{8,10},{9,11},{10,... | collective-permute-start | bytes 20 | tf_op jit(solution)/shard_map/ppermute | solution.py:41
  246.6 2.5 collective-permute-start.34
  249.6 3.4 collective-permute-start.35
  253.6 6.4 %collective-permute-start.36 = (f32[]{:T(128)}, f32[]{:T(128)}, u32[]{:S(2)}, u32[]{:S(2)}) collective-permute-start(f32[]{:T(128)} %max.49), channel_id=1, source_target_pairs={{0,16},{1,17},{2,18},{3,19},{4,20},{5,21},{6,22},{7,23},{8,24},{9,... | collective-permute-start | bytes 20 | tf_op jit(solution)/shard_map/ppermute | solution.py:41
  260.5 12.8 %collective-permute-start.37 = (f32[]{:T(128)}, f32[]{:T(128)}, u32[]{:S(2)}, u32[]{:S(2)}) collective-permute-start(f32[]{:T(128)} %max.50), channel_id=1, source_target_pairs={{0,32},{32,0},{64,96},{96,64},{128,160},{160,128},{192,224},{224,1... | collective-permute-start | bytes 20 | tf_op jit(solution)/shard_map/ppermute | solution.py:41
  273.9 2.5 collective-permute-start.38
  276.9 4.0 %collective-permute-start.39 = (f32[]{:T(128)}, f32[]{:T(128)}, u32[]{:S(2)}, u32[]{:S(2)}) collective-permute-start(f32[]{:T(128)} %max.52), channel_id=1, source_target_pairs={{0,128},{32,160},{64,192},{96,224},{128,0},{160,32},{192,64},{224,... | collective-permute-start | bytes 20 | tf_op jit(solution)/shard_map/ppermute | solution.py:41
  281.9 45.7 %collective-permute-start.29 = (f32[16,4,128]{2,1,0:T(4,128)S(1)}, f32[16,4,128]{2,1,0:T(4,128)S(1)}, u32[]{:S(2)}, u32[]{:S(2)}) collective-permute-start(f32[16,4,128]{2,1,0:T(4,128)S(1)} %constant_dynamic-slice_fusion.1), channel_id=1, source_target_pairs={{0,128},{32,160},{64,192},{96,224},{128,0},{160,32},{192,64},{224,... | collective-permute-start | bytes 98312 | tf_op jit(solution)/shard_map/ppermute | solution.py:71
  324.4 4.3 %collective-permute-start.43 = (f32[2,48,137]{1,2,0:T(8,128)S(1)}, f32[2,48,137]{1,2,0:T(8,128)S(1)}, u32[]{:S(2)}, u32[]{:S(2)}) collective-permute-start(f32[2,48,137]{1,2,0:T(8,128)S(1)} %concatenate.205), channel_id=1, source_target_pairs={{0,32},{32,0},{64,96},{96,64},{128,160},{160,128},{192,224},{224,1... | collective-permute-start | bytes 157832 | tf_op jit(solution)/shard_map/ppermute | solution.py:41
  327.7 3.7 %collective-permute-start.30 = (f32[2,16,4,128]{3,2,1,0:T(4,128)S(1)}, f32[2,16,4,128]{3,2,1,0:T(4,128)S(1)}, u32[]{:S(2)}, u32[]{:S(2)}) collective-permute-start(f32[2,16,4,128]{3,2,1,0:T(4,128)S(1)} %maximum_select_fusion.18), channel_id=1, source_target_pairs={{0,64},{32,96},{64,0},{96,32},{128,192},{160,224},{192,128},{224,1... | collective-permute-start | bytes 196616 | tf_op jit(solution)/shard_map/ppermute | solution.py:71
  328.7 5.9 %collective-permute-start.44 = (f32[2,48,137]{1,2,0:T(8,128)S(1)}, f32[2,48,137]{1,2,0:T(8,128)S(1)}, u32[]{:S(2)}, u32[]{:S(2)}) collective-permute-start(f32[2,48,137]{1,2,0:T(8,128)S(1)} %add.297), channel_id=1, source_target_pairs={{0,64},{32,96},{64,0},{96,32},{128,192},{160,224},{192,128},{224,1... | collective-permute-start | bytes 157832 | tf_op jit(solution)/shard_map/ppermute | solution.py:41
  331.4 10.7 %collective-permute-start.31 = (f32[2,2,16,4,128]{4,3,2,0,1:T(4,128)S(1)}, f32[2,2,16,4,128]{4,3,2,0,1:T(4,128)S(1)}, u32[]{:S(2)}, u32[]{:S(2)}) collective-permute-start(f32[2,2,16,4,128]{4,3,2,0,1:T(4,128)S(1)} %maximum_select_fusion.14), channel_id=1, source_target_pairs={{0,32},{32,0},{64,96},{96,64},{128,160},{160,128},{192,224},{224,1... | collective-permute-start | bytes 393224 | tf_op jit(solution)/shard_map/ppermute | solution.py:71
  334.7 6.2 %collective-permute-start.45 = (f32[2,48,137]{1,2,0:T(8,128)S(1)}, f32[2,48,137]{1,2,0:T(8,128)S(1)}, u32[]{:S(2)}, u32[]{:S(2)}) collective-permute-start(f32[2,48,137]{1,2,0:T(8,128)S(1)} %add.298), channel_id=1, source_target_pairs={{0,128},{32,160},{64,192},{96,224},{128,0},{160,32},{192,64},{224,... | collective-permute-start | bytes 157832 | tf_op jit(solution)/shard_map/ppermute | solution.py:41
  342.5 1.0 copy-start.2
